TPU v7x, 256 devices: a whole 4x4x8 slice. The times are simulated.
256 devices in a mesh: gx: 16 (over z, core), gy: 16 (over y, x).
Axes of the slice: x: 4, y: 4, z: 8, core: 2. Of those that a mesh axis runs over, the one named last changes fastest.
Arguments:
- right_side: float32 [256, 128, 1024], P('gx', 'gy'), may hold values from -340 to 340
- start_guess: float32 [256, 128, 1024], P('gx', 'gy'), may hold values from -1.8 to 1.8
- couple_x: float32 [256, 128, 64], P('gx', 'gy'), may hold values from 0.3 to 3
- couple_y: float32 [256, 128, 64], P('gx', 'gy'), may hold values from 0.3 to 3
- couple_z: float32 [256, 128, 64], P('gx', 'gy'), may hold values from 0.3 to 3
- reaction: float32 [256, 128, 64], P('gx', 'gy'), may hold values from 0.01 to 0.1
Outputs:
- solution: float32 [256, 128, 1024], P('gx', 'gy')
- residual: float32 [256, 128, 1024], P('gx', 'gy')
All inputs are finite; a program needn't handle non-finite values.
Results may differ from a plain program's by a relative error of at most 0.0003.
Values sent between devices are 32-bit elements; how exact they have to be, the bound alone decides.
No kernel may reach another device: no remote copies, remote signals or barrier semaphores. Data moves between devices by JAX's collectives and lax.ppermute only.
A program may use at most 64 MiB of HBM per device.

v0:
```python
import jax
import jax.numpy as jnp
from jax import lax
from jax.sharding import PartitionSpec as P

ITERS = 2
SWEEPS = 4
FACT_SWEEPS = 3


HIGH = lax.Precision.HIGHEST


def passed_along(block, axis, distance):
    devices = range(lax.axis_size(axis))
    route = [(i - distance, i) for i in devices if i - distance in devices]
    return lax.ppermute(block, axis, route)


def padded_2(block, sides, width):
    for axis, dim in sides:
        count = lax.axis_size(axis)
        forward = [(i, i + 1) for i in range(count - 1)]
        backward = [(target, source) for source, target in forward]
        low = lax.ppermute(
            lax.slice_in_dim(block, block.shape[dim] - width, None, axis=dim), axis, forward
        )
        high = lax.ppermute(lax.slice_in_dim(block, 0, width, axis=dim), axis, backward)
        block = jnp.concatenate([low, block, high], axis=dim)
    return block


def low_shift(values, along):
    count = values.shape[along]
    blank = jnp.zeros_like(lax.slice_in_dim(values, 0, 1, axis=along))
    return jnp.concatenate([blank, lax.slice_in_dim(values, 0, count - 1, axis=along)], axis=along)


def up_shift(values, along):
    count = values.shape[along]
    blank = jnp.zeros_like(lax.slice_in_dim(values, 0, 1, axis=along))
    return jnp.concatenate([lax.slice_in_dim(values, 1, count, axis=along), blank], axis=along)


def block_gram(former, latter, count_rhs):
    cells = former.shape[0] * former.shape[1]
    left = former.reshape(cells, count_rhs, -1)
    right = latter.reshape(cells, count_rhs, -1)
    return jnp.einsum("psz,ptz->st", left, right, precision=HIGH)


def mix_block(values, matrix):
    rows_x, rows_y, flat_len = values.shape
    count_rhs = matrix.shape[0]
    split = values.reshape(rows_x * rows_y, count_rhs, flat_len // count_rhs)
    return jnp.einsum("psz,st->ptz", split, matrix, precision=HIGH).reshape(
        rows_x, rows_y, flat_len
    )


def chol_factor(gram_mat):
    low_factor = jnp.linalg.cholesky(gram_mat)
    eye_mat = jnp.eye(gram_mat.shape[0], dtype=gram_mat.dtype)
    inverse = lax.linalg.triangular_solve(low_factor, eye_mat, left_side=True, lower=True)
    return (low_factor.T, inverse.T)


def solve_small(columns, first_factor):
    hessen = jnp.concatenate(columns, axis=1)
    count_rhs = first_factor.shape[0]
    target = jnp.dot(hessen[:count_rhs].T, first_factor, precision=HIGH)
    normal = jnp.dot(hessen.T, hessen, precision=HIGH)
    low_factor = jnp.linalg.cholesky(normal)
    partial_sol = lax.linalg.triangular_solve(low_factor, target, left_side=True, lower=True)
    return lax.linalg.triangular_solve(
        low_factor, partial_sol, left_side=True, lower=True, transpose_a=True
    )


def body(right_side, start_guess, couple_x, couple_y, couple_z, reaction):
    rows_x, rows_y, flat_len = right_side.shape
    layers = couple_z.shape[2]
    count_rhs = flat_len // layers
    depth = jnp.arange(flat_len, dtype=jnp.int32) % layers
    keep_first = (depth != 0).astype(jnp.float32)
    keep_last = (depth != layers - 1).astype(jnp.float32)

    def low_z(values):
        return low_shift(values, 2) * keep_first

    def up_z(values):
        return up_shift(values, 2) * keep_last

    def tiled(values):
        return jnp.tile(values, (1, 1, count_rhs))

    edge_x = passed_along(couple_x[-1:], "gx", 1)
    edge_y = passed_along(couple_y[:, -1:], "gy", 1)
    after_x = tiled(couple_x)
    after_y = tiled(couple_y)
    after_z = tiled(couple_z)
    before_x = tiled(jnp.concatenate([edge_x, couple_x[:-1]], axis=0))
    before_y = tiled(jnp.concatenate([edge_y, couple_y[:, :-1]], axis=1))
    before_z = low_z(after_z)
    diagonal = tiled(reaction) + after_x + before_x + after_y + before_y + after_z + before_z

    def apply_op(values):
        padded = padded_2(values, (("gx", 0), ("gy", 1)), 1)
        centre = padded[1:-1, 1:-1]
        return (
            diagonal * centre
            - after_x * padded[2:, 1:-1]
            - before_x * padded[:-2, 1:-1]
            - after_y * padded[1:-1, 2:]
            - before_y * padded[1:-1, :-2]
            - after_z * up_z(centre)
            - before_z * low_z(centre)
        )

    lows = (low_shift(after_x, 0), low_shift(after_y, 1), before_z)
    ups = (
        up_shift(jnp.ones_like(after_x), 0) * after_x,
        up_shift(jnp.ones_like(after_y), 1) * after_y,
        after_z,
    )
    pivots = diagonal
    for repeat in range(FACT_SWEEPS):
        inv_now = 1.0 / pivots
        pivots = (
            diagonal
            - lows[0] * lows[0] * low_shift(inv_now, 0)
            - lows[1] * lows[1] * low_shift(inv_now, 1)
            - lows[2] * lows[2] * low_z(inv_now)
        )
    inv_piv = 1.0 / pivots

    def total_gram(former, latter):
        return lax.psum(block_gram(former, latter, count_rhs), ("gx", "gy"))

    start_res = right_side - apply_op(start_guess)
    first_factor, first_inv = chol_factor(total_gram(start_res, start_res))
    basis_set = [mix_block(start_res, first_inv)]
    precond_set = []
    image_set = []
    columns = []
    for column in range(ITERS):
        source = basis_set[column]
        lower_sol = inv_piv * source
        for precondition_repeat in range(SWEEPS):
            lower_sol = inv_piv * (
                source
                + lows[0] * low_shift(lower_sol, 0)
                + lows[1] * low_shift(lower_sol, 1)
                + lows[2] * low_z(lower_sol)
            )
        upper_sol = lower_sol
        for precondition_repeat in range(SWEEPS):
            upper_sol = lower_sol + inv_piv * (
                ups[0] * up_shift(upper_sol, 0)
                + ups[1] * up_shift(upper_sol, 1)
                + ups[2] * up_z(upper_sol)
            )
        image = apply_op(upper_sol)
        precond_set.append(upper_sol)
        image_set.append(image)
        local_proj = jnp.stack([block_gram(member, image, count_rhs) for member in basis_set])
        stacked = lax.psum(local_proj, ("gx", "gy"))
        projections = [stacked[member] for member in range(len(basis_set))]
        removed = mix_block(basis_set[0], projections[0])
        for member in range(1, len(basis_set)):
            removed = removed + mix_block(basis_set[member], projections[member])
        perp = image - removed
        next_factor, next_inv = chol_factor(total_gram(perp, perp))
        if column + 1 < ITERS:
            basis_set.append(mix_block(perp, next_inv))
        blank = jnp.zeros(((ITERS - 1 - column) * count_rhs, count_rhs), dtype=next_factor.dtype)
        columns.append(jnp.concatenate(projections + [next_factor, blank], axis=0))
    coeffs = solve_small(columns, first_factor)
    solution = start_guess
    for column in range(ITERS):
        solution = solution + mix_block(
            precond_set[column], coeffs[column * count_rhs : (column + 1) * count_rhs]
        )
    residual = right_side - apply_op(solution)
    return (solution, residual)


def solution(mesh):
    return jax.shard_map(
        body,
        mesh=mesh,
        in_specs=(
            P("gx", "gy", None),
            P("gx", "gy", None),
            P("gx", "gy", None),
            P("gx", "gy", None),
            P("gx", "gy", None),
            P("gx", "gy", None),
        ),
        out_specs=(P("gx", "gy", None), P("gx", "gy", None)),
        check_vma=False,
    )
```

profile of v0, /device:TPU:40, one launch (start us, length us, event | category | flops | bytes accessed | tf_op | source)
XLA Modules:
  0.0 608.5 jit_solution(9430777300080090725)
XLA Ops:
  3.4 3.6 collective-permute-start.2
  9.3 3.4 collective-permute-start.1
  29.7 4.6 collective-permute-start.4
  39.6 3.6 collective-permute-done.5
  43.2 3.8 fusion.36
  49.3 3.1 convolution_bitcast_fusion.12
  57.6 77.3 %psum.35 = f32[16,16]{0,1:T(8,128)S(1)} all-reduce(f32[16,16]{0,1:T(8,128)S(1)} %convolution_bitcast_fusion.12), channel_id=1, replica_groups=mesh['gx'=16,'gy'=16] {'gx','gy'}, use_global_device_ids=true, to_apply=%region_0.1 | all-reduce | flops 256 | bytes 2048 | tf_op jit(solution)/shard_map/psum | solution.py:138
  153.0 2.8 collective-permute-start.6
  157.7 3.3 collective-permute-done.7
  161.1 4.6 collective-permute-start.8
  168.1 6.2 %collective-permute-done.9 = f32[18,1,1024]{2,1,0:T(1,128)S(1)} collective-permute-done((f32[18,1,1024]{2,1,0:T(1,128)S(1)}, f32[18,1,1024]{2,1,0:T(1,128)S(1)}, u32[]{:S(2)}, u32[]{:S(2)}) %collective-permute-start.9) | collective-permute-done | bytes 73760 | tf_op jit(solution)/shard_map/ppermute | solution.py:25
  182.5 71.4 %psum.36 = f32[16,16]{0,1:T(8,128)S(1)} all-reduce(f32[16,16]{0,1:T(8,128)S(1)} %convolution_bitcast_fusion.10), channel_id=1, replica_groups=mesh['gx'=16,'gy'=16] {'gx','gy'}, use_global_device_ids=true, to_apply=%region_3.6 | all-reduce | flops 256 | bytes 2048 | tf_op jit(solution)/shard_map/psum | solution.py:167
  268.0 3.1 convolution_bitcast_fusion.9
  271.0 74.0 %psum.37 = f32[16,16]{0,1:T(8,128)S(1)} all-reduce(f32[16,16]{0,1:T(8,128)S(1)} %convolution_bitcast_fusion.9), channel_id=1, replica_groups=mesh['gx'=16,'gy'=16] {'gx','gy'}, use_global_device_ids=true, to_apply=%region_4.7 | all-reduce | flops 256 | bytes 2048 | tf_op jit(solution)/shard_map/psum | solution.py:138
  364.9 2.9 collective-permute-start.10
  375.0 4.6 collective-permute-start.12
  388.1 2.9 fusion.15
  398.7 75.0 %psum.38 = f32[2,16,16]{1,2,0:T(8,128)S(1)} all-reduce(f32[2,16,16]{1,2,0:T(8,128)S(1)} %pad_maximum_fusion.39), channel_id=1, replica_groups=mesh['gx'=16,'gy'=16] {'gx','gy'}, use_global_device_ids=true, to_apply=%region_5.8 | all-reduce | flops 512 | bytes 4096 | tf_op jit(solution)/shard_map/psum | solution.py:167
  483.3 3.1 convolution_bitcast_fusion.5
  486.5 74.9 %psum.39 = f32[16,16]{0,1:T(8,128)S(1)} all-reduce(f32[16,16]{0,1:T(8,128)S(1)} %convolution_bitcast_fusion.5), channel_id=1, replica_groups=mesh['gx'=16,'gy'=16] {'gx','gy'}, use_global_device_ids=true, to_apply=%region_6.9 | all-reduce | flops 256 | bytes 2048 | tf_op jit(solution)/shard_map/psum | solution.py:138
  565.4 2.9 cholesky.41
  590.7 2.8 collective-permute-done.15
  593.6 4.7 collective-permute-start.16
  600.6 6.2 %collective-permute-done.17 = f32[18,1,1024]{2,1,0:T(1,128)S(1)} collective-permute-done((f32[18,1,1024]{2,1,0:T(1,128)S(1)}, f32[18,1,1024]{2,1,0:T(1,128)S(1)}, u32[]{:S(2)}, u32[]{:S(2)}) %collective-permute-start.17) | collective-permute-done | bytes 73760 | tf_op jit(solution)/shard_map/ppermute | solution.py:25
  (248 shorter events, 161.8 us)
Async XLA Ops:
  0.6 8.6 %copy-start.23 = (f32[16,8,64]{2,1,0:T(8,128)S(1)}, f32[16,8,64]{2,1,0:T(8,128)}, u32[]{:S(2)}) copy-start(f32[16,8,64]{2,1,0:T(8,128)} %param.12) | copy-start | bytes 98308
  1.5 27.3 %collective-permute-start.3 = (f32[1,8,1024]{2,1,0:T(8,128)S(1)}, f32[1,8,1024]{2,1,0:T(8,128)S(1)}, u32[]{:S(2)}, u32[]{:S(2)}) collective-permute-start(f32[1,8,1024]{2,1,0:T(8,128)S(1)} %get-tuple-element.31), channel_id=1, source_target_pairs={{0,16},{16,32},{32,48},{48,64},{64,80},{80,96},{96,112},{112,128},... | collective-permute-start | bytes 98312 | tf_op jit(solution)/shard_map/ppermute | solution.py:25
  3.4 25.4 %collective-permute-start.2 = (f32[1,8,1024]{2,1,0:T(8,128)S(1)}, f32[1,8,1024]{2,1,0:T(8,128)S(1)}, u32[]{:S(2)}, u32[]{:S(2)}) collective-permute-start(f32[1,8,1024]{2,1,0:T(8,128)S(1)} %get-tuple-element.30), channel_id=1, source_target_pairs={{16,0},{32,16},{48,32},{64,48},{80,64},{96,80},{112,96},{128,112},... | collective-permute-start | bytes 98312 | tf_op jit(solution)/shard_map/ppermute | solution.py:28
  7.1 18.2 %collective-permute-start = (f32[1,8,64]{2,1,0:T(8,128)S(1)}, f32[1,8,64]{2,1,0:T(8,128)S(1)}, u32[]{:S(2)}, u32[]{:S(2)}) collective-permute-start(f32[1,8,64]{2,1,0:T(8,128)S(1)} %slice.369), channel_id=1, source_target_pairs={{0,16},{16,32},{32,48},{48,64},{64,80},{80,96},{96,112},{112,128},... | collective-permute-start | bytes 6152 | tf_op jit(solution)/shard_map/ppermute | solution.py:17
  9.3 26.9 %collective-permute-start.1 = (f32[16,1,64]{2,1,0:T(1,128)S(1)}, f32[16,1,64]{2,1,0:T(1,128)S(1)}, u32[]{:S(2)}, u32[]{:S(2)}) collective-permute-start(f32[16,1,64]{2,1,0:T(1,128)S(1)} %slice.371), channel_id=1, source_target_pairs={{0,1},{1,2},{2,3},{3,4},{4,5},{5,6},{6,7},{7,8},{8,9},{9,10},{10,1... | collective-permute-start | bytes 12296 | tf_op jit(solution)/shard_map/ppermute | solution.py:17
  29.7 9.9 %collective-permute-start.4 = (f32[18,1,1024]{2,1,0:T(1,128)S(1)}, f32[18,1,1024]{2,1,0:T(1,128)S(1)}, u32[]{:S(2)}, u32[]{:S(2)}) collective-permute-start(f32[18,1,1024]{2,1,0:T(1,128)S(1)} %get-tuple-element.14), channel_id=1, source_target_pairs={{1,0},{2,1},{3,2},{4,3},{5,4},{6,5},{7,6},{8,7},{9,8},{10,9},{11,1... | collective-permute-start | bytes 221192 | tf_op jit(solution)/shard_map/ppermute | solution.py:28
  34.3 8.9 %collective-permute-start.5 = (f32[18,1,1024]{2,1,0:T(1,128)S(1)}, f32[18,1,1024]{2,1,0:T(1,128)S(1)}, u32[]{:S(2)}, u32[]{:S(2)}) collective-permute-start(f32[18,1,1024]{2,1,0:T(1,128)S(1)} %get-tuple-element.15), channel_id=1, source_target_pairs={{0,1},{1,2},{2,3},{3,4},{4,5},{5,6},{6,7},{7,8},{8,9},{9,10},{10,1... | collective-permute-start | bytes 221192 | tf_op jit(solution)/shard_map/ppermute | solution.py:25
  152.9 21.3 %copy-start = (f32[16,8,1024]{2,1,0:T(8,128)}, f32[16,8,1024]{2,1,0:T(8,128)S(1)}, u32[]{:S(2)}) copy-start(f32[16,8,1024]{2,1,0:T(8,128)S(1)} %multiply_add_fusion.4) | copy-start | bytes 1572868
  153.0 4.8 collective-permute-start.6
  155.8 5.2 collective-permute-start.7
  161.1 6.9 %collective-permute-start.8 = (f32[18,1,1024]{2,1,0:T(1,128)S(1)}, f32[18,1,1024]{2,1,0:T(1,128)S(1)}, u32[]{:S(2)}, u32[]{:S(2)}) collective-permute-start(f32[18,1,1024]{2,1,0:T(1,128)S(1)} %get-tuple-element.12), channel_id=1, source_target_pairs={{1,0},{2,1},{3,2},{4,3},{5,4},{6,5},{7,6},{8,7},{9,8},{10,9},{11,1... | collective-permute-start | bytes 221192 | tf_op jit(solution)/shard_map/ppermute | solution.py:28
  165.8 8.5 %collective-permute-start.9 = (f32[18,1,1024]{2,1,0:T(1,128)S(1)}, f32[18,1,1024]{2,1,0:T(1,128)S(1)}, u32[]{:S(2)}, u32[]{:S(2)}) collective-permute-start(f32[18,1,1024]{2,1,0:T(1,128)S(1)} %get-tuple-element.13), channel_id=1, source_target_pairs={{0,1},{1,2},{2,3},{3,4},{4,5},{5,6},{6,7},{7,8},{8,9},{9,10},{10,1... | collective-permute-start | bytes 221192 | tf_op jit(solution)/shard_map/ppermute | solution.py:25
  364.9 10.0 %collective-permute-start.10 = (f32[1,8,1024]{2,1,0:T(8,128)S(1)}, f32[1,8,1024]{2,1,0:T(8,128)S(1)}, u32[]{:S(2)}, u32[]{:S(2)}) collective-permute-start(f32[1,8,1024]{2,1,0:T(8,128)S(1)} %get-tuple-element.23), channel_id=1, source_target_pairs={{16,0},{32,16},{48,32},{64,48},{80,64},{96,80},{112,96},{128,112},... | collective-permute-start | bytes 98312 | tf_op jit(solution)/shard_map/ppermute | solution.py:28
  367.9 7.0 %collective-permute-start.11 = (f32[1,8,1024]{2,1,0:T(8,128)S(1)}, f32[1,8,1024]{2,1,0:T(8,128)S(1)}, u32[]{:S(2)}, u32[]{:S(2)}) collective-permute-start(f32[1,8,1024]{2,1,0:T(8,128)S(1)} %get-tuple-element.22), channel_id=1, source_target_pairs={{0,16},{16,32},{32,48},{48,64},{64,80},{80,96},{96,112},{112,128},... | collective-permute-start | bytes 98312 | tf_op jit(solution)/shard_map/ppermute | solution.py:25
  375.0 11.5 %collective-permute-start.12 = (f32[18,1,1024]{2,1,0:T(1,128)S(1)}, f32[18,1,1024]{2,1,0:T(1,128)S(1)}, u32[]{:S(2)}, u32[]{:S(2)}) collective-permute-start(f32[18,1,1024]{2,1,0:T(1,128)S(1)} %get-tuple-element.10), channel_id=1, source_target_pairs={{1,0},{2,1},{3,2},{4,3},{5,4},{6,5},{7,6},{8,7},{9,8},{10,9},{11,1... | collective-permute-start | bytes 221192 | tf_op jit(solution)/shard_map/ppermute | solution.py:28
  379.6 8.4 %collective-permute-start.13 = (f32[18,1,1024]{2,1,0:T(1,128)S(1)}, f32[18,1,1024]{2,1,0:T(1,128)S(1)}, u32[]{:S(2)}, u32[]{:S(2)}) collective-permute-start(f32[18,1,1024]{2,1,0:T(1,128)S(1)} %get-tuple-element.11), channel_id=1, source_target_pairs={{0,1},{1,2},{2,3},{3,4},{4,5},{5,6},{6,7},{7,8},{8,9},{9,10},{10,1... | collective-permute-start | bytes 221192 | tf_op jit(solution)/shard_map/ppermute | solution.py:25
  483.3 89.2 %copy-start.20 = (f32[128,16,64]{0,1,2:T(8,128)S(1)}, f32[128,16,64]{0,1,2:T(8,128)}, u32[]{:S(2)}) copy-start(f32[128,16,64]{0,1,2:T(8,128)} %copy.56) | copy-start | bytes 1572868
  586.3 20.5 %copy-start.9 = (f32[16,8,1024]{2,1,0:T(8,128)}, f32[16,8,1024]{2,1,0:T(8,128)S(1)}, u32[]{:S(2)}) copy-start(f32[16,8,1024]{2,1,0:T(8,128)S(1)} %add_add_fusion) | copy-start | bytes 1572868
  586.3 4.3 collective-permute-start.14
  588.3 5.2 collective-permute-start.15
  593.6 7.0 %collective-permute-start.16 = (f32[18,1,1024]{2,1,0:T(1,128)S(1)}, f32[18,1,1024]{2,1,0:T(1,128)S(1)}, u32[]{:S(2)}, u32[]{:S(2)}) collective-permute-start(f32[18,1,1024]{2,1,0:T(1,128)S(1)} %get-tuple-element.8), channel_id=1, source_target_pairs={{1,0},{2,1},{3,2},{4,3},{5,4},{6,5},{7,6},{8,7},{9,8},{10,9},{11,1... | collective-permute-start | bytes 221192 | tf_op jit(solution)/shard_map/ppermute | solution.py:28
  598.2 8.5 %copy-start.11 = (f32[16,8,1024]{2,1,0:T(8,128)S(1)}, f32[16,8,1024]{2,1,0:T(8,128)}, u32[]{:S(2)}) copy-start(f32[16,8,1024]{2,1,0:T(8,128)} %tile.63) | copy-start | bytes 1572868
  598.3 8.5 %copy-start.13 = (f32[16,8,1024]{2,1,0:T(8,128)S(1)}, f32[16,8,1024]{2,1,0:T(8,128)}, u32[]{:S(2)}) copy-start(f32[16,8,1024]{2,1,0:T(8,128)} %tile.67) | copy-start | bytes 1572868
  598.3 8.5 %collective-permute-start.17 = (f32[18,1,1024]{2,1,0:T(1,128)S(1)}, f32[18,1,1024]{2,1,0:T(1,128)S(1)}, u32[]{:S(2)}, u32[]{:S(2)}) collective-permute-start(f32[18,1,1024]{2,1,0:T(1,128)S(1)} %get-tuple-element.9), channel_id=1, source_target_pairs={{0,1},{1,2},{2,3},{3,4},{4,5},{5,6},{6,7},{7,8},{8,9},{9,10},{10,1... | collective-permute-start | bytes 221192 | tf_op jit(solution)/shard_map/ppermute | solution.py:25
  (21 other events, 59.9 us)
where the time goes:
time: 617 us; the launch traced here: 609 us
  blocking collectives  373 us (60%)
  local copies, waits for them, and re-layouts  87.7 us (14%)
  starting transfers between devices  51.7 us (8%)
  other arithmetic  44.9 us (7%)
  matrix products  26 us (4%)
  waiting for transfers between devices  23.7 us (4%)
    psum x3, blocking collectives, total_gram(): return lax.psum(block_gram(former, latter, count_rhs), ('gx', 'gy'))  226 us
    psum x2, blocking collectives, body(): stacked = lax.psum(local_proj, ('gx', 'gy'))  146 us
    ppermute x8, starting transfers between devices, padded_2(): lax.ppermute(lax.slice_in_dim(block, 0, width, axis=dim), axis, backward)  29.8 us
    ppermute x8, waiting for transfers between devices, padded_2(): lax.ppermute(lax.slice_in_dim(block, block.shape[dim] - width, None, axis...  23.7 us
    ppermute x8, starting transfers between devices, padded_2(): lax.ppermute(lax.slice_in_dim(block, block.shape[dim] - width, None, axis...  16.3 us
    another operation x14, local copies, waits for them, and re-layouts, tiled(): return jnp.tile(values, (1, 1, count_rhs))  16.1 us
    dot_general x6, matrix products, block_gram(): return jnp.einsum('psz,ptz->st', left, right, precision=HIGH)  14 us
  transfers between devices with their start and end apart: 18, of which 6 were waited for; matrix products, arithmetic and copies ran while one was open for 5% of the time, Pallas kernels for 0%

commit v1 on v0

--- a/solution.py
+++ b/solution.py
@@ -15,6 +15,26 @@
     devices = range(lax.axis_size(axis))
     route = [(i - distance, i) for i in devices if i - distance in devices]
     return lax.ppermute(block, axis, route)
+
+
+def mesh_sum(block):
+    for axis in ("gx", "gy"):
+        count = lax.axis_size(axis)
+        if count & (count - 1):
+            block = lax.psum(block, axis)
+            continue
+        step = 1
+        while step < count:
+            radix = 4 if count % (step * 4) == 0 else 2
+            parts = [block] + [
+                lax.ppermute(block, axis, [(i, i ^ (step * m)) for i in range(count)])
+                for m in range(1, radix)
+            ]
+            while len(parts) > 1:
+                parts = [parts[i] + parts[i + 1] for i in range(0, len(parts), 2)]
+            block = parts[0]
+            step *= radix
+    return block
 
 
 def padded_2(block, sides, width):
@@ -135,7 +155,7 @@
     inv_piv = 1.0 / pivots
 
     def total_gram(former, latter):
-        return lax.psum(block_gram(former, latter, count_rhs), ("gx", "gy"))
+        return mesh_sum(block_gram(former, latter, count_rhs))
 
     start_res = right_side - apply_op(start_guess)
     first_factor, first_inv = chol_factor(total_gram(start_res, start_res))
@@ -164,7 +184,7 @@
         precond_set.append(upper_sol)
         image_set.append(image)
         local_proj = jnp.stack([block_gram(member, image, count_rhs) for member in basis_set])
-        stacked = lax.psum(local_proj, ("gx", "gy"))
+        stacked = mesh_sum(local_proj)
         projections = [stacked[member] for member in range(len(basis_set))]
         removed = mix_block(basis_set[0], projections[0])
         for member in range(1, len(basis_set)):

time: 617 us -> 385 us (0.62)
  blocking collectives: 373 us -> 0 us
  starting transfers between devices: 51.7 us -> 150 us
  waiting for transfers between devices: 23.7 us -> 79.8 us
  local copies, waits for them, and re-layouts: 87.7 us -> 78.9 us
    psum x5 -> x0, blocking collectives: 373 us -> none  [the longest x3 226 us: total_gram(): return lax.psum(block_gram(former, latter, count_rhs), ('gx', 'gy'))]
    ppermute x0 -> x60, starting transfers between devices: none -> 97.2 us  [mesh_sum(): lax.ppermute(block, axis, [(i, i ^ step * m) for i in range(count)])]
    ppermute x0 -> x60, waiting for transfers between devices: none -> 49.1 us  [mesh_sum(): lax.ppermute(block, axis, [(i, i ^ step * m) for i in range(count)])]
    ppermute x8, waiting for transfers between devices: 23.7 us -> 30.7 us  [padded_2(): lax.ppermute(lax.slice_in_dim(block, block.shape[dim] - width, None, axis...]
  transfers between devices with their start and end apart: 18 -> 78, of which waited for: 6 -> 36; matrix products, arithmetic and copies ran while one was open for 5% -> 7% of each run, Pallas kernels for 0% -> 0%
where the time goes in v1:
time: 385 us; the launch traced here: 378 us
  starting transfers between devices  150 us (39%)
  waiting for transfers between devices  79.8 us (21%)
  local copies, waits for them, and re-layouts  78.9 us (20%)
  other arithmetic  42.4 us (11%)
  matrix products  25.3 us (7%)
    ppermute x60, starting transfers between devices, mesh_sum(): lax.ppermute(block, axis, [(i, i ^ step * m) for i in range(count)])  97.2 us
    ppermute x60, waiting for transfers between devices, mesh_sum(): lax.ppermute(block, axis, [(i, i ^ step * m) for i in range(count)])  49.1 us
    ppermute x8, waiting for transfers between devices, padded_2(): lax.ppermute(lax.slice_in_dim(block, block.shape[dim] - width, None, axis...  30.7 us
    ppermute x8, starting transfers between devices, padded_2(): lax.ppermute(lax.slice_in_dim(block, 0, width, axis=dim), axis, backward)  29.7 us
    ppermute x8, starting transfers between devices, padded_2(): lax.ppermute(lax.slice_in_dim(block, block.shape[dim] - width, None, axis...  17.2 us
    dot_general x6, matrix products, block_gram(): return jnp.einsum('psz,ptz->st', left, right, precision=HIGH)  12.4 us
    reshape x5, local copies, waits for them, and re-layouts, mix_block(): jnp.einsum('psz,st->ptz', split, matrix, precision=HIGH)  11.7 us
    transpose x5, local copies, waits for them, and re-layouts, mix_block(): jnp.einsum('psz,st->ptz', split, matrix, precision=HIGH)  11.4 us
  transfers between devices with their start and end apart: 78, of which 36 were waited for; matrix products, arithmetic and copies ran while one was open for 7% of the time, Pallas kernels for 0%

profile of v1, /device:TPU:40, one launch (start us, length us, event | category | flops | bytes accessed | tf_op | source)
XLA Modules:
  0.0 378.1 jit_solution(18006876973593988738)
XLA Ops:
  3.4 3.6 collective-permute-start.2
  9.3 3.4 collective-permute-start.1
  22.6 4.6 %collective-permute-start.4 = (f32[18,1,1024]{2,1,0:T(1,128)S(1)}, f32[18,1,1024]{2,1,0:T(1,128)S(1)}, u32[]{:S(2)}, u32[]{:S(2)}) collective-permute-start(f32[18,1,1024]{2,1,0:T(1,128)S(1)} %get-tuple-element.14), channel_id=1, source_target_pairs={{1,0},{2,1},{3,2},{4,3},{5,4},{6,5},{7,6},{8,7},{9,8},{10,9},{11,1... | collective-permute-start | bytes 221192 | tf_op jit(solution)/shard_map/ppermute | solution.py:48
  32.5 3.6 collective-permute-done.5
  36.7 3.7 fusion.36
  47.7 6.3 %collective-permute-start.10 = (f32[16,16]{0,1:T(8,128)S(1)}, f32[16,16]{0,1:T(8,128)S(1)}, u32[]{:S(2)}, u32[]{:S(2)}) collective-permute-start(f32[16,16]{0,1:T(8,128)S(1)} %add_add_fusion.21), channel_id=1, source_target_pairs={{0,128},{16,144},{32,160},{48,176},{64,192},{80,208},{96,224},{112... | collective-permute-start | bytes 3080 | tf_op jit(solution)/shard_map/ppermute | solution.py:30
  56.2 3.6 collective-permute-done.11
  60.6 3.6 collective-permute-start.13
  102.2 4.8 %collective-permute-start.20 = (f32[18,1,1024]{2,1,0:T(1,128)S(1)}, f32[18,1,1024]{2,1,0:T(1,128)S(1)}, u32[]{:S(2)}, u32[]{:S(2)}) collective-permute-start(f32[18,1,1024]{2,1,0:T(1,128)S(1)} %get-tuple-element.12), channel_id=1, source_target_pairs={{1,0},{2,1},{3,2},{4,3},{5,4},{6,5},{7,6},{8,7},{9,8},{10,9},{11,1... | collective-permute-start | bytes 221192 | tf_op jit(solution)/shard_map/ppermute | solution.py:48
  109.3 6.2 %collective-permute-done.21 = f32[18,1,1024]{2,1,0:T(1,128)S(1)} collective-permute-done((f32[18,1,1024]{2,1,0:T(1,128)S(1)}, f32[18,1,1024]{2,1,0:T(1,128)S(1)}, u32[]{:S(2)}, u32[]{:S(2)}) %collective-permute-start.21) | collective-permute-done | bytes 73760 | tf_op jit(solution)/shard_map/ppermute | solution.py:45
  123.9 10.3 %collective-permute-start.24 = (f32[1,16,16]{1,2,0:T(8,128)S(1)}, f32[1,16,16]{1,2,0:T(8,128)S(1)}, u32[]{:S(2)}, u32[]{:S(2)}) collective-permute-start(f32[1,16,16]{1,2,0:T(8,128)S(1)} %convolution_bitcast_fusion.10), channel_id=1, source_target_pairs={{0,48},{16,32},{32,16},{48,0},{64,112},{80,96},{96,80},{112,64},{1... | collective-permute-start | bytes 3080 | tf_op jit(solution)/shard_map/ppermute | solution.py:30
  137.4 4.1 %collective-permute-start.26 = (f32[1,16,16]{1,2,0:T(8,128)S(1)}, f32[1,16,16]{1,2,0:T(8,128)S(1)}, u32[]{:S(2)}, u32[]{:S(2)}) collective-permute-start(f32[1,16,16]{1,2,0:T(8,128)S(1)} %add_add_fusion.17), channel_id=1, source_target_pairs={{0,128},{16,144},{32,160},{48,176},{64,192},{80,208},{96,224},{112... | collective-permute-start | bytes 3080 | tf_op jit(solution)/shard_map/ppermute | solution.py:30
  147.4 4.6 %collective-permute-start.30 = (f32[1,16,16]{1,2,0:T(8,128)S(1)}, f32[1,16,16]{1,2,0:T(8,128)S(1)}, u32[]{:S(2)}, u32[]{:S(2)}) collective-permute-start(f32[1,16,16]{1,2,0:T(8,128)S(1)} %add_add_fusion.16), channel_id=1, source_target_pairs={{0,3},{1,2},{2,1},{3,0},{4,7},{5,6},{6,5},{7,4},{8,11},{9,10},{10,... | collective-permute-start | bytes 3080 | tf_op jit(solution)/shard_map/ppermute | solution.py:30
  187.3 4.1 %collective-permute-start.41 = (f32[16,16]{0,1:T(8,128)S(1)}, f32[16,16]{0,1:T(8,128)S(1)}, u32[]{:S(2)}, u32[]{:S(2)}) collective-permute-start(f32[16,16]{0,1:T(8,128)S(1)} %add_add_fusion.12), channel_id=1, source_target_pairs={{0,2},{1,3},{2,0},{3,1},{4,6},{5,7},{6,4},{7,5},{8,10},{9,11},{10,... | collective-permute-start | bytes 3080 | tf_op jit(solution)/shard_map/ppermute | solution.py:30
  230.6 4.1 %collective-permute-start.48 = (f32[18,1,1024]{2,1,0:T(1,128)S(1)}, f32[18,1,1024]{2,1,0:T(1,128)S(1)}, u32[]{:S(2)}, u32[]{:S(2)}) collective-permute-start(f32[18,1,1024]{2,1,0:T(1,128)S(1)} %get-tuple-element.10), channel_id=1, source_target_pairs={{1,0},{2,1},{3,2},{4,3},{5,4},{6,5},{7,6},{8,7},{9,8},{10,9},{11,1... | collective-permute-start | bytes 221192 | tf_op jit(solution)/shard_map/ppermute | solution.py:48
  237.0 6.2 %collective-permute-done.49 = f32[18,1,1024]{2,1,0:T(1,128)S(1)} collective-permute-done((f32[18,1,1024]{2,1,0:T(1,128)S(1)}, f32[18,1,1024]{2,1,0:T(1,128)S(1)}, u32[]{:S(2)}, u32[]{:S(2)}) %collective-permute-start.49) | collective-permute-done | bytes 73760 | tf_op jit(solution)/shard_map/ppermute | solution.py:45
  257.0 4.1 %collective-permute-start.54 = (f32[2,16,16]{1,2,0:T(8,128)S(1)}, f32[2,16,16]{1,2,0:T(8,128)S(1)}, u32[]{:S(2)}, u32[]{:S(2)}) collective-permute-start(f32[2,16,16]{1,2,0:T(8,128)S(1)} %add_add_fusion.5), channel_id=1, source_target_pairs={{0,128},{16,144},{32,160},{48,176},{64,192},{80,208},{96,224},{112... | collective-permute-start | bytes 6152 | tf_op jit(solution)/shard_map/ppermute | solution.py:30
  267.4 4.6 %collective-permute-start.58 = (f32[2,16,16]{1,2,0:T(8,128)S(1)}, f32[2,16,16]{1,2,0:T(8,128)S(1)}, u32[]{:S(2)}, u32[]{:S(2)}) collective-permute-start(f32[2,16,16]{1,2,0:T(8,128)S(1)} %add_add_fusion.4), channel_id=1, source_target_pairs={{0,3},{1,2},{2,1},{3,0},{4,7},{5,6},{6,5},{7,4},{8,11},{9,10},{10,... | collective-permute-start | bytes 6152 | tf_op jit(solution)/shard_map/ppermute | solution.py:30
  303.9 3.8 collective-permute-done.66
  308.6 3.8 %collective-permute-start.69 = (f32[16,16]{0,1:T(8,128)S(1)}, f32[16,16]{0,1:T(8,128)S(1)}, u32[]{:S(2)}, u32[]{:S(2)}) collective-permute-start(f32[16,16]{0,1:T(8,128)S(1)} %add_add_fusion.8), channel_id=1, source_target_pairs={{0,2},{1,3},{2,0},{3,1},{4,6},{5,7},{6,4},{7,5},{8,10},{9,11},{10,... | collective-permute-start | bytes 3080 | tf_op jit(solution)/shard_map/ppermute | solution.py:30
  319.4 3.3 collective-permute-start.71
  324.3 3.5 collective-permute-done.72
  361.1 6.8 %collective-permute-start.76 = (f32[18,1,1024]{2,1,0:T(1,128)S(1)}, f32[18,1,1024]{2,1,0:T(1,128)S(1)}, u32[]{:S(2)}, u32[]{:S(2)}) collective-permute-start(f32[18,1,1024]{2,1,0:T(1,128)S(1)} %get-tuple-element.8), channel_id=1, source_target_pairs={{1,0},{2,1},{3,2},{4,3},{5,4},{6,5},{7,6},{8,7},{9,8},{10,9},{11,1... | collective-permute-start | bytes 221192 | tf_op jit(solution)/shard_map/ppermute | solution.py:48
  370.2 6.2 %collective-permute-done.77 = f32[18,1,1024]{2,1,0:T(1,128)S(1)} collective-permute-done((f32[18,1,1024]{2,1,0:T(1,128)S(1)}, f32[18,1,1024]{2,1,0:T(1,128)S(1)}, u32[]{:S(2)}, u32[]{:S(2)}) %collective-permute-start.77) | collective-permute-done | bytes 73760 | tf_op jit(solution)/shard_map/ppermute | solution.py:45
  (391 shorter events, 263.0 us)
Async XLA Ops:
  1.5 20.0 %collective-permute-start.3 = (f32[1,8,1024]{2,1,0:T(8,128)S(1)}, f32[1,8,1024]{2,1,0:T(8,128)S(1)}, u32[]{:S(2)}, u32[]{:S(2)}) collective-permute-start(f32[1,8,1024]{2,1,0:T(8,128)S(1)} %get-tuple-element.31), channel_id=1, source_target_pairs={{0,16},{16,32},{32,48},{48,64},{64,80},{80,96},{96,112},{112,128},... | collective-permute-start | bytes 98312 | tf_op jit(solution)/shard_map/ppermute | solution.py:45
  3.4 18.2 %collective-permute-start.2 = (f32[1,8,1024]{2,1,0:T(8,128)S(1)}, f32[1,8,1024]{2,1,0:T(8,128)S(1)}, u32[]{:S(2)}, u32[]{:S(2)}) collective-permute-start(f32[1,8,1024]{2,1,0:T(8,128)S(1)} %get-tuple-element.30), channel_id=1, source_target_pairs={{16,0},{32,16},{48,32},{64,48},{80,64},{96,80},{112,96},{128,112},... | collective-permute-start | bytes 98312 | tf_op jit(solution)/shard_map/ppermute | solution.py:48
  7.1 11.8 %collective-permute-start = (f32[1,8,64]{2,1,0:T(8,128)S(1)}, f32[1,8,64]{2,1,0:T(8,128)S(1)}, u32[]{:S(2)}, u32[]{:S(2)}) collective-permute-start(f32[1,8,64]{2,1,0:T(8,128)S(1)} %slice.369), channel_id=1, source_target_pairs={{0,16},{16,32},{32,48},{48,64},{64,80},{80,96},{96,112},{112,128},... | collective-permute-start | bytes 6152 | tf_op jit(solution)/shard_map/ppermute | solution.py:17
  9.3 19.8 %collective-permute-start.1 = (f32[16,1,64]{2,1,0:T(1,128)S(1)}, f32[16,1,64]{2,1,0:T(1,128)S(1)}, u32[]{:S(2)}, u32[]{:S(2)}) collective-permute-start(f32[16,1,64]{2,1,0:T(1,128)S(1)} %slice.371), channel_id=1, source_target_pairs={{0,1},{1,2},{2,3},{3,4},{4,5},{5,6},{6,7},{7,8},{8,9},{9,10},{10,1... | collective-permute-start | bytes 12296 | tf_op jit(solution)/shard_map/ppermute | solution.py:17
  22.6 9.9 %collective-permute-start.4 = (f32[18,1,1024]{2,1,0:T(1,128)S(1)}, f32[18,1,1024]{2,1,0:T(1,128)S(1)}, u32[]{:S(2)}, u32[]{:S(2)}) collective-permute-start(f32[18,1,1024]{2,1,0:T(1,128)S(1)} %get-tuple-element.14), channel_id=1, source_target_pairs={{1,0},{2,1},{3,2},{4,3},{5,4},{6,5},{7,6},{8,7},{9,8},{10,9},{11,1... | collective-permute-start | bytes 221192 | tf_op jit(solution)/shard_map/ppermute | solution.py:48
  27.1 8.9 %collective-permute-start.5 = (f32[18,1,1024]{2,1,0:T(1,128)S(1)}, f32[18,1,1024]{2,1,0:T(1,128)S(1)}, u32[]{:S(2)}, u32[]{:S(2)}) collective-permute-start(f32[18,1,1024]{2,1,0:T(1,128)S(1)} %get-tuple-element.15), channel_id=1, source_target_pairs={{0,1},{1,2},{2,3},{3,4},{4,5},{5,6},{6,7},{7,8},{8,9},{9,10},{10,1... | collective-permute-start | bytes 221192 | tf_op jit(solution)/shard_map/ppermute | solution.py:45
  47.7 8.5 %collective-permute-start.10 = (f32[16,16]{0,1:T(8,128)S(1)}, f32[16,16]{0,1:T(8,128)S(1)}, u32[]{:S(2)}, u32[]{:S(2)}) collective-permute-start(f32[16,16]{0,1:T(8,128)S(1)} %add_add_fusion.21), channel_id=1, source_target_pairs={{0,128},{16,144},{32,160},{48,176},{64,192},{80,208},{96,224},{112... | collective-permute-start | bytes 3080 | tf_op jit(solution)/shard_map/ppermute | solution.py:30
  69.1 7.7 %collective-permute-start.15 = (f32[16,16]{0,1:T(8,128)S(1)}, f32[16,16]{0,1:T(8,128)S(1)}, u32[]{:S(2)}, u32[]{:S(2)}) collective-permute-start(f32[16,16]{0,1:T(8,128)S(1)} %add_add_fusion.19), channel_id=1, source_target_pairs={{0,4},{1,5},{2,6},{3,7},{4,0},{5,1},{6,2},{7,3},{8,12},{9,13},{10,... | collective-permute-start | bytes 3080 | tf_op jit(solution)/shard_map/ppermute | solution.py:30
  69.5 7.2 %collective-permute-start.16 = (f32[16,16]{0,1:T(8,128)S(1)}, f32[16,16]{0,1:T(8,128)S(1)}, u32[]{:S(2)}, u32[]{:S(2)}) collective-permute-start(f32[16,16]{0,1:T(8,128)S(1)} %add_add_fusion.19), channel_id=1, source_target_pairs={{0,8},{1,9},{2,10},{3,11},{4,12},{5,13},{6,14},{7,15},{8,0},{9,1},... | collective-permute-start | bytes 3080 | tf_op jit(solution)/shard_map/ppermute | solution.py:30
  102.2 7.1 %collective-permute-start.20 = (f32[18,1,1024]{2,1,0:T(1,128)S(1)}, f32[18,1,1024]{2,1,0:T(1,128)S(1)}, u32[]{:S(2)}, u32[]{:S(2)}) collective-permute-start(f32[18,1,1024]{2,1,0:T(1,128)S(1)} %get-tuple-element.12), channel_id=1, source_target_pairs={{1,0},{2,1},{3,2},{4,3},{5,4},{6,5},{7,6},{8,7},{9,8},{10,9},{11,1... | collective-permute-start | bytes 221192 | tf_op jit(solution)/shard_map/ppermute | solution.py:48
  107.0 8.5 %collective-permute-start.21 = (f32[18,1,1024]{2,1,0:T(1,128)S(1)}, f32[18,1,1024]{2,1,0:T(1,128)S(1)}, u32[]{:S(2)}, u32[]{:S(2)}) collective-permute-start(f32[18,1,1024]{2,1,0:T(1,128)S(1)} %get-tuple-element.13), channel_id=1, source_target_pairs={{0,1},{1,2},{2,3},{3,4},{4,5},{5,6},{6,7},{7,8},{8,9},{9,10},{10,1... | collective-permute-start | bytes 221192 | tf_op jit(solution)/shard_map/ppermute | solution.py:45
  123.8 10.5 %collective-permute-start.22 = (f32[1,16,16]{1,2,0:T(8,128)S(1)}, f32[1,16,16]{1,2,0:T(8,128)S(1)}, u32[]{:S(2)}, u32[]{:S(2)}) collective-permute-start(f32[1,16,16]{1,2,0:T(8,128)S(1)} %convolution_bitcast_fusion.10), channel_id=1, source_target_pairs={{0,16},{16,0},{32,48},{48,32},{64,80},{80,64},{96,112},{112,96},{1... | collective-permute-start | bytes 3080 | tf_op jit(solution)/shard_map/ppermute | solution.py:30
  123.8 10.4 %collective-permute-start.23 = (f32[1,16,16]{1,2,0:T(8,128)S(1)}, f32[1,16,16]{1,2,0:T(8,128)S(1)}, u32[]{:S(2)}, u32[]{:S(2)}) collective-permute-start(f32[1,16,16]{1,2,0:T(8,128)S(1)} %convolution_bitcast_fusion.10), channel_id=1, source_target_pairs={{0,32},{16,48},{32,0},{48,16},{64,96},{80,112},{96,64},{112,80},{1... | collective-permute-start | bytes 3080 | tf_op jit(solution)/shard_map/ppermute | solution.py:30
  123.9 12.0 %collective-permute-start.24 = (f32[1,16,16]{1,2,0:T(8,128)S(1)}, f32[1,16,16]{1,2,0:T(8,128)S(1)}, u32[]{:S(2)}, u32[]{:S(2)}) collective-permute-start(f32[1,16,16]{1,2,0:T(8,128)S(1)} %convolution_bitcast_fusion.10), channel_id=1, source_target_pairs={{0,48},{16,32},{32,16},{48,0},{64,112},{80,96},{96,80},{112,64},{1... | collective-permute-start | bytes 3080 | tf_op jit(solution)/shard_map/ppermute | solution.py:30
  137.4 7.6 %collective-permute-start.26 = (f32[1,16,16]{1,2,0:T(8,128)S(1)}, f32[1,16,16]{1,2,0:T(8,128)S(1)}, u32[]{:S(2)}, u32[]{:S(2)}) collective-permute-start(f32[1,16,16]{1,2,0:T(8,128)S(1)} %add_add_fusion.17), channel_id=1, source_target_pairs={{0,128},{16,144},{32,160},{48,176},{64,192},{80,208},{96,224},{112... | collective-permute-start | bytes 3080 | tf_op jit(solution)/shard_map/ppermute | solution.py:30
  178.4 7.6 %collective-permute-start.38 = (f32[16,16]{0,1:T(8,128)S(1)}, f32[16,16]{0,1:T(8,128)S(1)}, u32[]{:S(2)}, u32[]{:S(2)}) collective-permute-start(f32[16,16]{0,1:T(8,128)S(1)} %add_add_fusion.13), channel_id=1, source_target_pairs={{0,128},{16,144},{32,160},{48,176},{64,192},{80,208},{96,224},{112... | collective-permute-start | bytes 3080 | tf_op jit(solution)/shard_map/ppermute | solution.py:30
  196.3 7.0 %collective-permute-start.43 = (f32[16,16]{0,1:T(8,128)S(1)}, f32[16,16]{0,1:T(8,128)S(1)}, u32[]{:S(2)}, u32[]{:S(2)}) collective-permute-start(f32[16,16]{0,1:T(8,128)S(1)} %add_add_fusion.11), channel_id=1, source_target_pairs={{0,4},{1,5},{2,6},{3,7},{4,0},{5,1},{6,2},{7,3},{8,12},{9,13},{10,... | collective-permute-start | bytes 3080 | tf_op jit(solution)/shard_map/ppermute | solution.py:30
  234.7 8.5 %collective-permute-start.49 = (f32[18,1,1024]{2,1,0:T(1,128)S(1)}, f32[18,1,1024]{2,1,0:T(1,128)S(1)}, u32[]{:S(2)}, u32[]{:S(2)}) collective-permute-start(f32[18,1,1024]{2,1,0:T(1,128)S(1)} %get-tuple-element.11), channel_id=1, source_target_pairs={{0,1},{1,2},{2,3},{3,4},{4,5},{5,6},{6,7},{7,8},{8,9},{9,10},{10,1... | collective-permute-start | bytes 221192 | tf_op jit(solution)/shard_map/ppermute | solution.py:45
  257.0 7.7 %collective-permute-start.54 = (f32[2,16,16]{1,2,0:T(8,128)S(1)}, f32[2,16,16]{1,2,0:T(8,128)S(1)}, u32[]{:S(2)}, u32[]{:S(2)}) collective-permute-start(f32[2,16,16]{1,2,0:T(8,128)S(1)} %add_add_fusion.5), channel_id=1, source_target_pairs={{0,128},{16,144},{32,160},{48,176},{64,192},{80,208},{96,224},{112... | collective-permute-start | bytes 6152 | tf_op jit(solution)/shard_map/ppermute | solution.py:30
  300.0 7.7 %collective-permute-start.66 = (f32[16,16]{0,1:T(8,128)S(1)}, f32[16,16]{0,1:T(8,128)S(1)}, u32[]{:S(2)}, u32[]{:S(2)}) collective-permute-start(f32[16,16]{0,1:T(8,128)S(1)} %add_add_fusion.9), channel_id=1, source_target_pairs={{0,128},{16,144},{32,160},{48,176},{64,192},{80,208},{96,224},{112... | collective-permute-start | bytes 3080 | tf_op jit(solution)/shard_map/ppermute | solution.py:30
  307.7 11.6 %collective-permute-start.68 = (f32[16,16]{0,1:T(8,128)S(1)}, f32[16,16]{0,1:T(8,128)S(1)}, u32[]{:S(2)}, u32[]{:S(2)}) collective-permute-start(f32[16,16]{0,1:T(8,128)S(1)} %add_add_fusion.8), channel_id=1, source_target_pairs={{0,1},{1,0},{2,3},{3,2},{4,5},{5,4},{6,7},{7,6},{8,9},{9,8},{10,11... | collective-permute-start | bytes 3080 | tf_op jit(solution)/shard_map/ppermute | solution.py:30
  308.6 10.8 %collective-permute-start.69 = (f32[16,16]{0,1:T(8,128)S(1)}, f32[16,16]{0,1:T(8,128)S(1)}, u32[]{:S(2)}, u32[]{:S(2)}) collective-permute-start(f32[16,16]{0,1:T(8,128)S(1)} %add_add_fusion.8), channel_id=1, source_target_pairs={{0,2},{1,3},{2,0},{3,1},{4,6},{5,7},{6,4},{7,5},{8,10},{9,11},{10,... | collective-permute-start | bytes 3080 | tf_op jit(solution)/shard_map/ppermute | solution.py:30
  361.1 9.1 %collective-permute-start.76 = (f32[18,1,1024]{2,1,0:T(1,128)S(1)}, f32[18,1,1024]{2,1,0:T(1,128)S(1)}, u32[]{:S(2)}, u32[]{:S(2)}) collective-permute-start(f32[18,1,1024]{2,1,0:T(1,128)S(1)} %get-tuple-element.8), channel_id=1, source_target_pairs={{1,0},{2,1},{3,2},{4,3},{5,4},{6,5},{7,6},{8,7},{9,8},{10,9},{11,1... | collective-permute-start | bytes 221192 | tf_op jit(solution)/shard_map/ppermute | solution.py:48
  367.9 8.5 %collective-permute-start.77 = (f32[18,1,1024]{2,1,0:T(1,128)S(1)}, f32[18,1,1024]{2,1,0:T(1,128)S(1)}, u32[]{:S(2)}, u32[]{:S(2)}) collective-permute-start(f32[18,1,1024]{2,1,0:T(1,128)S(1)} %get-tuple-element.9), channel_id=1, source_target_pairs={{0,1},{1,2},{2,3},{3,4},{4,5},{5,6},{6,7},{7,8},{8,9},{9,10},{10,1... | collective-permute-start | bytes 221192 | tf_op jit(solution)/shard_map/ppermute | solution.py:45
  (85 other events, 493.2 us)
